TPU v7x, 256 devices: a whole 4x4x8 slice. The times are simulated.
256 devices in a mesh: seq: 32 (over x, z), head: 8 (over y, core).
Axes of the slice: x: 4, y: 4, z: 8, core: 2. Of those that a mesh axis runs over, the one named last changes fastest.
Arguments:
- att_query: bfloat16 [8192, 16, 128], P('seq', 'head'), may hold values from -9 to 9
- att_key: bfloat16 [8192, 16, 128], P('seq', 'head'), may hold values from -9 to 9
- att_value: bfloat16 [8192, 16, 128], P('seq', 'head'), may hold values from -6 to 6
- norm_gain: float32 [16, 128], P('head'), may hold values from 0.1 to 1.9
- dn_query: bfloat16 [8192, 16, 128], P('seq', 'head'), may hold values from -6 to 6
- dn_key: bfloat16 [8192, 16, 128], P('seq', 'head'), may hold values from -4 to 4
- write_rate: float32 [8192, 16], P('seq', 'head'), may hold values from 0.04 to 0.9
- log_decay: float32 [8192, 16], P('seq', 'head'), may hold values from -1 to 0
- out_grad: bfloat16 [8192, 16, 128], P('seq', 'head'), may hold values from -6 to 6
Outputs:
- block_out: bfloat16 [8192, 16, 128], P('seq', 'head')
- att_query_grad: bfloat16 [8192, 16, 128], P('seq', 'head')
- att_key_grad: bfloat16 [8192, 16, 128], P('seq', 'head')
- att_value_grad: bfloat16 [8192, 16, 128], P('seq', 'head')
- gain_grad: float32 [16, 128], P('head')
- dn_query_grad: bfloat16 [8192, 16, 128], P('seq', 'head')
- dn_key_grad: bfloat16 [8192, 16, 128], P('seq', 'head')
- rate_grad: float32 [8192, 16], P('seq', 'head')
- decay_grad: float32 [8192, 16], P('seq', 'head')
All inputs are finite; a program needn't handle non-finite values.
Results may differ from a plain program's by a relative error of at most 0.018.
Values may be sent and summed in bfloat16 or wider, within the bound.
No kernel may reach another device: no remote copies, remote signals or barrier semaphores. Data moves between devices by JAX's collectives and lax.ppermute only.
A program may use at most 64 MiB of HBM per device.

v0:
```python
import jax
import jax.numpy as jnp
from jax import lax
from jax.sharding import PartitionSpec as P

WIN = 1024
CH = 64
MATMUL_ACCURACY = lax.Precision.HIGHEST
EPSILON = 1e-06


def shifted_2(block, axis, distance):
    devices = range(lax.axis_size(axis))
    route = [(i - distance, i) for i in devices if i - distance in devices]
    return lax.ppermute(block, axis, route)


def unit_rows(matrix):
    return matrix * lax.rsqrt(jnp.sum(matrix * matrix, axis=-1, keepdims=True) + EPSILON)


def delta_block(memory_state, pieces):
    query_vectors, key_vectors, value_rows, rate_rows, decay_rows = pieces
    length = key_vectors.shape[1]
    lower = jnp.tril(jnp.ones((length, length), jnp.float32))
    strict = lower - jnp.eye(length, dtype=jnp.float32)
    running_state = jnp.cumsum(decay_rows, axis=1)
    ratio = jnp.exp((running_state[:, :, None] - running_state[:, None, :]) * lower) * lower
    state_increment = jnp.exp(running_state)
    intersection = jnp.einsum("htk,hsk->hts", key_vectors, key_vectors, precision=MATMUL_ACCURACY)
    system = (
        jnp.eye(length, dtype=jnp.float32) + rate_rows[:, :, None] * ratio * strict * intersection
    )
    retrieved_values = jnp.einsum(
        "nex,nxp->nep", key_vectors, memory_state, precision=MATMUL_ACCURACY
    )
    target = rate_rows[:, :, None] * (value_rows - state_increment[:, :, None] * retrieved_values)
    newest_state = jax.scipy.linalg.solve_triangular(system, target, lower=True, unit_diagonal=True)
    local_scores = (
        jnp.einsum("htk,hsk->hts", query_vectors, key_vectors, precision=MATMUL_ACCURACY) * ratio
    )
    state_output = state_increment[:, :, None] * jnp.einsum(
        "nex,nxp->nep", query_vectors, memory_state, precision=MATMUL_ACCURACY
    )
    state_output = state_output + jnp.einsum(
        "hts,hsv->htv", local_scores, newest_state, precision=MATMUL_ACCURACY
    )
    retained_state = jnp.exp(running_state[:, -1:] - running_state)
    memory_state = jnp.exp(running_state[:, -1])[:, None, None] * memory_state + jnp.einsum(
        "wpa,wpn->wan",
        key_vectors * retained_state[:, :, None],
        newest_state,
        precision=MATMUL_ACCURACY,
    )
    return (memory_state, state_output)


def delta_sweep(memory_state, query_vectors, key_vectors, value_rows, rate_rows, decay_rows):
    head_count, length = (key_vectors.shape[0], key_vectors.shape[1])
    blocks = length // CH

    def cut_blocks(array):
        return jnp.moveaxis(array.reshape((head_count, blocks, CH) + array.shape[2:]), 1, 0)

    last_state, state_output = lax.scan(
        delta_block,
        memory_state,
        (
            cut_blocks(query_vectors),
            cut_blocks(key_vectors),
            cut_blocks(value_rows),
            cut_blocks(rate_rows),
            cut_blocks(decay_rows),
        ),
    )
    return (
        last_state,
        jnp.moveaxis(state_output, 0, 1).reshape(head_count, length, state_output.shape[-1]),
    )


def window_softmax(rows_here, keys_here, values_here, alive_keys):
    block_rows = rows_here.shape[0]
    span_rows = keys_here.shape[0]
    reach_back = span_rows - block_rows
    scores = jnp.einsum("qhd,khd->hqk", rows_here, keys_here) * rows_here.shape[-1] ** (-0.5)
    query_pos = jnp.arange(block_rows, dtype=jnp.int32)[:, None]
    key_pos = jnp.arange(span_rows, dtype=jnp.int32)[None, :]
    allowed = (key_pos > query_pos) & (key_pos <= query_pos + reach_back) & alive_keys[None, :]
    scores = jnp.where(allowed[None], scores, -1e30)
    shifted = jnp.exp(scores - jnp.max(scores, axis=-1, keepdims=True))
    weights_bf = (shifted / jnp.sum(shifted, axis=-1, keepdims=True)).astype(jnp.bfloat16)
    return jnp.einsum("hqk,khd->qhd", weights_bf.astype(jnp.float32), values_here)


def attend(query_vectors, key_vectors, value_rows, alive_keys):
    outputs = [window_softmax(query_vectors, key_vectors, value_rows, alive_keys)]
    return jnp.concatenate(outputs, axis=0)


def apply_map(matrix, operand):
    return jnp.einsum("hij,hjv->hiv", matrix, operand, precision=MATMUL_ACCURACY)


def body(
    att_query, att_key, att_value, norm_gain, dn_query, dn_key, write_rate, log_decay, out_grad
):
    row_count, head_count, head_width = att_query.shape
    rim_rows = min(WIN, row_count)
    reach_back = max(1, WIN // row_count)
    my_shard = lax.axis_index("seq")
    shard_count = lax.axis_size("seq")
    older_keys = []
    older_values = []
    for offset in range(reach_back):
        came_key, came_value = shifted_2((att_key, att_value), "seq", offset + 1)
        older_keys.insert(0, came_key)
        older_values.insert(0, came_value)
    all_keys = jnp.concatenate(older_keys + [att_key], axis=0).astype(jnp.float32)
    all_values = jnp.concatenate(older_values + [att_value], axis=0).astype(jnp.float32)
    alive_keys = my_shard * row_count - WIN + jnp.arange(WIN + row_count, dtype=jnp.int32) >= 0

    def attention_core(query_vectors, key_vectors, value_rows):
        return attend(query_vectors, key_vectors, value_rows, alive_keys)

    attended, attention_pull = jax.vjp(
        attention_core, att_query.astype(jnp.float32), all_keys, all_values
    )
    square_part = jnp.sum(attended * attended, axis=(1, 2))
    square_all = lax.psum(square_part, "head")
    features = head_count * lax.axis_size("head") * head_width
    inverse = lax.rsqrt(square_all / features + EPSILON)
    scaled = attended * inverse[:, None, None]
    values = (scaled * norm_gain[None]).astype(jnp.bfloat16)
    query_heads = jnp.swapaxes(dn_query, 0, 1).astype(jnp.float32)
    key_heads = jnp.swapaxes(dn_key, 0, 1).astype(jnp.float32)
    value_heads = jnp.swapaxes(values, 0, 1)
    rate_heads = write_rate.T
    decay_heads = log_decay.T
    identity = jnp.broadcast_to(
        jnp.eye(head_width, dtype=jnp.float32), (head_count, head_width, head_width)
    )
    seed_state = jnp.concatenate(
        [identity, jnp.zeros((head_count, head_width, head_width), jnp.float32)], axis=-1
    )
    folded_values = jnp.concatenate(
        [jnp.zeros(value_heads.shape, jnp.float32), value_heads.astype(jnp.float32)], axis=-1
    )
    summary, unused_out = delta_sweep(
        seed_state,
        unit_rows(query_heads),
        unit_rows(key_heads),
        folded_values,
        rate_heads,
        decay_heads,
    )
    carry_map = summary[..., :head_width]
    carry_add = summary[..., head_width:]
    empty_state = jnp.zeros_like(carry_add)

    def relay(turn, current):
        return shifted_2(apply_map(carry_map, current) + carry_add, "seq", 1)

    start_state = lax.fori_loop(0, shard_count - 1, relay, empty_state)

    def local_delta(start_in, query_in, key_in, value_in, rate_in, decay_in):
        last_state, state_output = delta_sweep(
            start_in,
            unit_rows(query_in),
            unit_rows(key_in),
            value_in.astype(jnp.float32),
            rate_in,
            decay_in,
        )
        return (state_output, last_state)

    (state_output, last_state), delta_pull = jax.vjp(
        local_delta, start_state, query_heads, key_heads, value_heads, rate_heads, decay_heads
    )
    cotangent = jnp.swapaxes(out_grad, 0, 1).astype(jnp.float32)
    own_back = delta_pull((cotangent, empty_state))[0]
    flipped = jnp.swapaxes(carry_map, 1, 2)

    def relay_back(turn, current):
        return shifted_2(apply_map(flipped, current) + own_back, "seq", -1)

    later_grad = lax.fori_loop(0, shard_count - 1, relay_back, empty_state)
    delta_grads = delta_pull((cotangent, later_grad))
    value_grad = jnp.swapaxes(delta_grads[3], 0, 1).astype(jnp.float32)
    weighted = value_grad * norm_gain[None]
    dot_part = jnp.sum(weighted * attended, axis=(1, 2))
    gain_part = jnp.sum(value_grad * scaled, axis=0)
    dot_all = lax.psum(dot_part, "head")
    gain_grad = lax.psum(gain_part, "seq")
    attended_grad = (
        inverse[:, None, None] * weighted
        - attended * (inverse * inverse * inverse * dot_all / features)[:, None, None]
    )
    query_grad, keys_grad, values_grad = attention_pull(attended_grad)
    own_key_grad = keys_grad[WIN:]
    own_value_grad = values_grad[WIN:]
    extra_key = jnp.zeros((rim_rows, head_count, head_width), jnp.float32)
    extra_value = jnp.zeros((rim_rows, head_count, head_width), jnp.float32)
    for offset in range(reach_back):
        segment = reach_back - 1 - offset
        sent_key = keys_grad[segment * rim_rows : (segment + 1) * rim_rows]
        sent_value = values_grad[segment * rim_rows : (segment + 1) * rim_rows]
        came_key, came_value = (
            shifted_2(sent_key.astype(jnp.bfloat16), "seq", -(offset + 1)).astype(sent_key.dtype),
            shifted_2(sent_value.astype(jnp.bfloat16), "seq", -(offset + 1)).astype(
                sent_value.dtype
            ),
        )
        extra_key = extra_key + came_key
        extra_value = extra_value + came_value
    own_key_grad = own_key_grad.at[row_count - rim_rows :].add(extra_key)
    own_value_grad = own_value_grad.at[row_count - rim_rows :].add(extra_value)
    block_out = jnp.swapaxes(state_output, 0, 1).astype(jnp.bfloat16)
    return (
        block_out,
        query_grad.astype(jnp.bfloat16),
        own_key_grad.astype(jnp.bfloat16),
        own_value_grad.astype(jnp.bfloat16),
        gain_grad,
        jnp.swapaxes(delta_grads[1], 0, 1).astype(jnp.bfloat16),
        jnp.swapaxes(delta_grads[2], 0, 1).astype(jnp.bfloat16),
        delta_grads[4].T,
        delta_grads[5].T,
    )


def solution(mesh):
    return jax.shard_map(
        body,
        mesh=mesh,
        in_specs=(
            P("seq", "head", None),
            P("seq", "head", None),
            P("seq", "head", None),
            P("head", None),
            P("seq", "head", None),
            P("seq", "head", None),
            P("seq", "head"),
            P("seq", "head"),
            P("seq", "head", None),
        ),
        out_specs=(
            P("seq", "head", None),
            P("seq", "head", None),
            P("seq", "head", None),
            P("seq", "head", None),
            P("head", None),
            P("seq", "head", None),
            P("seq", "head", None),
            P("seq", "head"),
            P("seq", "head"),
        ),
        check_vma=False,
    )
```

profile of v0, /device:TPU:162, one launch (start us, length us, event | category | flops | bytes accessed | tf_op | source)
XLA Modules:
  0.0 1278.0 jit_solution(2413856035602274087)
XLA Ops:
  59.0 14.4 %psum.21 = f32[256]{0:T(256)S(1)} all-reduce(f32[256]{0:T(256)S(1)} %get-tuple-element.2481), channel_id=1, replica_groups=mesh['seq'=32,'head'=8] {'head'}, use_global_device_ids=true, to_apply=%region_4.5 | all-reduce | flops 256 | bytes 2048 | tf_op jit(solution)/shard_map/psum | solution.py:130
  78.7 69.7 %while.136 = (s32[]{:T(128)}, f32[2,128,256]{2,1,0:T(8,128)S(1)}, f32[4,2,64]{2,1,0:T(2,128)}, f32[4,2,64,128]{3,2,1,0:T(8,128)S(1)}, f32[4,2,64]{2,1,0:T(2,128)...) while((s32[]{:T(128)}, f32[2,128,256]{2,1,0:T(8,128)S(1)}, f32[4,2,64]{2,1,0:T(2,128)}, ...), condition=%wide.region_7.8_spmd, body=%wide.region_5.0_spmd.sunk | while | flops 138780736 | bytes 1925833 | solution.py:65
  82.6 11.2 custom-call.55
  100.0 11.2 custom-call.55
  117.4 11.2 custom-call.55
  134.9 11.2 custom-call.55
  152.2 311.7 %while.137 = (s32[]{:T(128)}, f32[2,128,128]{2,1,0:T(8,128)S(1)}, f32[2,128,128]{2,1,0:T(8,128)S(1)}, f32[2,128,128]{2,1,0:T(8,128)S(1)}, s32[]{:T(128)}) while((s32[]{:T(128)}, f32[2,128,128]{2,1,0:T(8,128)S(1)}, f32[2,128,128]{2,1,0:T(8,128)S(1)}, f32[2,128,128]{2,1,0:T(8,128)S(1)}, s32[]{:T(128)}) %tuple.298), condition=%wide.region_9.10_spmd, body=%wide.region_8.9_spmd.sunk | while | flops 50364416 | bytes 1048677 | solution.py:164
  467.6 105.8 %while.139 = (s32[]{:T(128)}, f32[2,128,128]{2,1,0:T(8,128)S(1)}, bf16[4,2,64,128]{3,2,1,0:T(8,128)(2,1)}, f32[4,2,64,64]{3,2,1,0:T(8,128)}, f32[4,2,64]{2,1,0:T...) while((s32[]{:T(128)}, f32[2,128,128]{2,1,0:T(8,128)S(1)}, ...), condition=%wide.region_13.14_spmd.clone.clone, body=%wide.region_11.13_spmd.clone.clone.sunk | while | flops 126304576 | bytes 3452789 | solution.py:65
  472.0 10.6 custom-call.56
  498.4 10.6 custom-call.56
  524.8 10.6 custom-call.56
  551.3 10.6 custom-call.56
  574.0 65.0 %while.141 = (s32[]{:T(128)}, f32[2,128,128]{2,1,0:T(8,128)S(1)}, f32[4,2,1,1]{1,3,2,0:T(1,128)}, f32[4,2,64,128]{3,2,1,0:T(8,128)}, f32[4,2,64,1]{2,1,3,0:T(2,1...) while((s32[]{:T(128)}, f32[2,128,128]{2,1,0:T(8,128)S(1)}, ...), condition=%wide.region_15.17_spmd.clone, body=%wide.region_14.16_spmd.clone.sunk | while | flops 100937792 | bytes 1587911 | solution.py:65
  577.7 9.8 custom-call.59
  594.0 9.8 custom-call.59
  610.2 9.8 custom-call.59
  626.5 9.8 custom-call.59
  639.0 292.8 %while.138 = (s32[]{:T(128)}, f32[2,128,128]{2,1,0:T(8,128)S(1)}, f32[2,128,128]{2,1,0:T(8,128)S(1)}, f32[2,128,128]{2,1,0:T(8,128)S(1)}, s32[]{:T(128)}) while((s32[]{:T(128)}, f32[2,128,128]{2,1,0:T(8,128)S(1)}, f32[2,128,128]{2,1,0:T(8,128)S(1)}, f32[2,128,128]{2,1,0:T(8,128)S(1)}, s32[]{:T(128)}) %tuple.319), condition=%wide.region_17.19_spmd, body=%wide.region_16.18_spmd.sunk | while | flops 50364416 | bytes 1048677 | solution.py:187
  812.3 8.7 collective-permute-done.1
  935.1 192.5 %while.140 = (s32[]{:T(128)}, f32[2,128,128]{2,1,0:T(8,128)S(1)}, f32[4,2,64,128]{3,2,1,0:T(8,128)}, f32[4,2,64,128]{3,2,1,0:T(8,128)}, bf16[4,2,64,128]{3,2,0,1...) while((s32[]{:T(128)}, f32[2,128,128]{2,1,0:T(8,128)S(1)}, ...), condition=%wide.region_29.31_spmd.clone.clone, body=%wide.region_18.30_spmd.clone.clone.sunk | while | flops 258761408 | bytes 5408265 | solution.py:65
  939.3 9.8 custom-call.58
  953.5 9.8 custom-call.57
  987.4 9.8 custom-call.58
  1001.6 9.8 custom-call.57
  1035.5 9.8 custom-call.58
  1049.7 9.8 custom-call.57
  1083.6 9.8 custom-call.58
  1097.8 9.8 custom-call.57
  1130.5 12.4 psum.22
  1161.3 13.9 %collective-permute-start.16 = (bf16[256,2,128]{0,2,1:T(8,128)(2,1)S(1)}, bf16[256,2,128]{0,2,1:T(8,128)(2,1)S(1)}, u32[]{:S(2)}, u32[]{:S(2)}) collective-permute-start(bf16[256,2,128]{0,2,1:T(8,128)(2,1)S(1)} %get-tuple-element.2471), channel_id=1, source_target_pairs={{24,0},{32,8},{40,16},{48,24},{56,32},{64,40},{72,48},{80,56},{88,... | collective-permute-start | bytes 393224 | tf_op jit(solution)/shard_map/ppermute | solution.py:15
  1179.9 67.6 %psum.23 = f32[2,128]{1,0:T(2,128)} all-reduce(f32[2,128]{1,0:T(2,128)S(1)} %copy-done.42), channel_id=1, replica_groups=mesh['seq'=32,'head'=8] {'seq'}, use_global_device_ids=true, to_apply=%region_36.38 | all-reduce | flops 256 | bytes 2048 | tf_op jit(solution)/shard_map/psum | solution.py:194
  1253.7 10.1 collective-permute-start.12
  (769 shorter events, 941.7 us)
Async XLA Ops:
  1.7 32.5 %collective-permute-start.6 = (bf16[256,2,128]{2,0,1:T(8,128)(2,1)S(1)}, bf16[256,2,128]{2,0,1:T(8,128)(2,1)S(1)}, u32[]{:S(2)}, u32[]{:S(2)}) collective-permute-start(bf16[256,2,128]{2,0,1:T(8,128)(2,1)S(1)} %copy.247), channel_id=1, source_target_pairs={{0,32},{8,40},{16,48},{24,56},{32,64},{40,72},{48,80},{56,88},{64,... | collective-permute-start | bytes 393224 | tf_op jit(solution)/shard_map/ppermute | solution.py:15
  4.2 36.0 %collective-permute-start.7 = (bf16[256,2,128]{2,0,1:T(8,128)(2,1)S(1)}, bf16[256,2,128]{2,0,1:T(8,128)(2,1)S(1)}, u32[]{:S(2)}, u32[]{:S(2)}) collective-permute-start(bf16[256,2,128]{2,0,1:T(8,128)(2,1)S(1)} %copy.247), channel_id=1, source_target_pairs={{0,24},{8,32},{16,40},{24,48},{32,56},{40,64},{48,72},{56,80},{64,... | collective-permute-start | bytes 393224 | tf_op jit(solution)/shard_map/ppermute | solution.py:15
  11.9 30.7 %collective-permute-start.8 = (bf16[256,2,128]{2,0,1:T(8,128)(2,1)S(1)}, bf16[256,2,128]{2,0,1:T(8,128)(2,1)S(1)}, u32[]{:S(2)}, u32[]{:S(2)}) collective-permute-start(bf16[256,2,128]{2,0,1:T(8,128)(2,1)S(1)} %copy.247), channel_id=1, source_target_pairs={{0,16},{8,24},{16,32},{24,40},{32,48},{40,56},{48,64},{56,72},{64,... | collective-permute-start | bytes 393224 | tf_op jit(solution)/shard_map/ppermute | solution.py:15
  15.3 29.8 %collective-permute-start.9 = (bf16[256,2,128]{2,0,1:T(8,128)(2,1)S(1)}, bf16[256,2,128]{2,0,1:T(8,128)(2,1)S(1)}, u32[]{:S(2)}, u32[]{:S(2)}) collective-permute-start(bf16[256,2,128]{2,0,1:T(8,128)(2,1)S(1)} %copy.247), channel_id=1, source_target_pairs={{0,8},{8,16},{16,24},{24,32},{32,40},{40,48},{48,56},{56,64},{64,7... | collective-permute-start | bytes 393224 | tf_op jit(solution)/shard_map/ppermute | solution.py:15
  30.2 17.6 %collective-permute-start.2 = (bf16[256,2,128]{0,2,1:T(8,128)(2,1)S(1)}, bf16[256,2,128]{0,2,1:T(8,128)(2,1)S(1)}, u32[]{:S(2)}, u32[]{:S(2)}) collective-permute-start(bf16[256,2,128]{0,2,1:T(8,128)(2,1)S(1)} %copy.242), channel_id=1, source_target_pairs={{0,32},{8,40},{16,48},{24,56},{32,64},{40,72},{48,80},{56,88},{64,... | collective-permute-start | bytes 393224 | tf_op jit(solution)/shard_map/ppermute | solution.py:15
  34.2 15.9 %collective-permute-start.3 = (bf16[256,2,128]{0,2,1:T(8,128)(2,1)S(1)}, bf16[256,2,128]{0,2,1:T(8,128)(2,1)S(1)}, u32[]{:S(2)}, u32[]{:S(2)}) collective-permute-start(bf16[256,2,128]{0,2,1:T(8,128)(2,1)S(1)} %copy.242), channel_id=1, source_target_pairs={{0,24},{8,32},{16,40},{24,48},{32,56},{40,64},{48,72},{56,80},{64,... | collective-permute-start | bytes 393224 | tf_op jit(solution)/shard_map/ppermute | solution.py:15
  40.2 16.7 %collective-permute-start.4 = (bf16[256,2,128]{0,2,1:T(8,128)(2,1)S(1)}, bf16[256,2,128]{0,2,1:T(8,128)(2,1)S(1)}, u32[]{:S(2)}, u32[]{:S(2)}) collective-permute-start(bf16[256,2,128]{0,2,1:T(8,128)(2,1)S(1)} %copy.242), channel_id=1, source_target_pairs={{0,16},{8,24},{16,32},{24,40},{32,48},{40,56},{48,64},{56,72},{64,... | collective-permute-start | bytes 393224 | tf_op jit(solution)/shard_map/ppermute | solution.py:15
  42.6 15.2 %collective-permute-start.5 = (bf16[256,2,128]{0,2,1:T(8,128)(2,1)S(1)}, bf16[256,2,128]{0,2,1:T(8,128)(2,1)S(1)}, u32[]{:S(2)}, u32[]{:S(2)}) collective-permute-start(bf16[256,2,128]{0,2,1:T(8,128)(2,1)S(1)} %copy.242), channel_id=1, source_target_pairs={{0,8},{8,16},{16,24},{24,32},{32,40},{40,48},{48,56},{56,64},{64,7... | collective-permute-start | bytes 393224 | tf_op jit(solution)/shard_map/ppermute | solution.py:15
  198.9 9.5 collective-permute-start
  238.9 9.2 collective-permute-start
  279.3 9.9 collective-permute-start
  290.1 10.5 collective-permute-start
  362.2 9.6 collective-permute-start
  372.8 10.6 collective-permute-start
  639.2 9.3 collective-permute-start.1
  648.8 9.3 collective-permute-start.1
  658.4 9.4 collective-permute-start.1
  668.0 10.5 collective-permute-start.1
  678.8 10.1 collective-permute-start.1
  734.5 9.6 collective-permute-start.1
  744.3 10.3 collective-permute-start.1
  754.9 9.3 collective-permute-start.1
  810.4 10.6 collective-permute-start.1
  821.2 9.7 collective-permute-start.1
  1157.4 93.6 %collective-permute-start.14 = (bf16[256,2,128]{0,2,1:T(8,128)(2,1)S(1)}, bf16[256,2,128]{0,2,1:T(8,128)(2,1)S(1)}, u32[]{:S(2)}, u32[]{:S(2)}) collective-permute-start(bf16[256,2,128]{0,2,1:T(8,128)(2,1)S(1)} %get-tuple-element.2469), channel_id=1, source_target_pairs={{8,0},{16,8},{24,16},{32,24},{40,32},{48,40},{56,48},{64,56},{72,6... | collective-permute-start | bytes 393224 | tf_op jit(solution)/shard_map/ppermute | solution.py:15
  1159.4 94.3 %collective-permute-start.15 = (bf16[256,2,128]{0,2,1:T(8,128)(2,1)S(1)}, bf16[256,2,128]{0,2,1:T(8,128)(2,1)S(1)}, u32[]{:S(2)}, u32[]{:S(2)}) collective-permute-start(bf16[256,2,128]{0,2,1:T(8,128)(2,1)S(1)} %get-tuple-element.2472), channel_id=1, source_target_pairs={{16,0},{24,8},{32,16},{40,24},{48,32},{56,40},{64,48},{72,56},{80,... | collective-permute-start | bytes 393224 | tf_op jit(solution)/shard_map/ppermute | solution.py:15
  1161.3 102.5 %collective-permute-start.16 = (bf16[256,2,128]{0,2,1:T(8,128)(2,1)S(1)}, bf16[256,2,128]{0,2,1:T(8,128)(2,1)S(1)}, u32[]{:S(2)}, u32[]{:S(2)}) collective-permute-start(bf16[256,2,128]{0,2,1:T(8,128)(2,1)S(1)} %get-tuple-element.2471), channel_id=1, source_target_pairs={{24,0},{32,8},{40,16},{48,24},{56,32},{64,40},{72,48},{80,56},{88,... | collective-permute-start | bytes 393224 | tf_op jit(solution)/shard_map/ppermute | solution.py:15
  1175.2 90.5 %collective-permute-start.17 = (bf16[256,2,128]{0,2,1:T(8,128)(2,1)S(1)}, bf16[256,2,128]{0,2,1:T(8,128)(2,1)S(1)}, u32[]{:S(2)}, u32[]{:S(2)}) collective-permute-start(bf16[256,2,128]{0,2,1:T(8,128)(2,1)S(1)} %get-tuple-element.2470), channel_id=1, source_target_pairs={{32,0},{40,8},{48,16},{56,24},{64,32},{72,40},{80,48},{88,56},{96,... | collective-permute-start | bytes 393224 | tf_op jit(solution)/shard_map/ppermute | solution.py:15
  1177.2 90.4 %collective-permute-start.10 = (bf16[256,2,128]{2,0,1:T(8,128)(2,1)S(1)}, bf16[256,2,128]{2,0,1:T(8,128)(2,1)S(1)}, u32[]{:S(2)}, u32[]{:S(2)}) collective-permute-start(bf16[256,2,128]{2,0,1:T(8,128)(2,1)S(1)} %get-tuple-element.2473), channel_id=1, source_target_pairs={{8,0},{16,8},{24,16},{32,24},{40,32},{48,40},{56,48},{64,56},{72,6... | collective-permute-start | bytes 393224 | tf_op jit(solution)/shard_map/ppermute | solution.py:15
  1251.0 16.5 %collective-permute-start.11 = (bf16[256,2,128]{2,0,1:T(8,128)(2,1)S(1)}, bf16[256,2,128]{2,0,1:T(8,128)(2,1)S(1)}, u32[]{:S(2)}, u32[]{:S(2)}) collective-permute-start(bf16[256,2,128]{2,0,1:T(8,128)(2,1)S(1)} %get-tuple-element.2476), channel_id=1, source_target_pairs={{16,0},{24,8},{32,16},{40,24},{48,32},{56,40},{64,48},{72,56},{80,... | collective-permute-start | bytes 393224 | tf_op jit(solution)/shard_map/ppermute | solution.py:15
  1253.7 13.9 %collective-permute-start.12 = (bf16[256,2,128]{2,0,1:T(8,128)(2,1)S(1)}, bf16[256,2,128]{2,0,1:T(8,128)(2,1)S(1)}, u32[]{:S(2)}, u32[]{:S(2)}) collective-permute-start(bf16[256,2,128]{2,0,1:T(8,128)(2,1)S(1)} %get-tuple-element.2475), channel_id=1, source_target_pairs={{24,0},{32,8},{40,16},{48,24},{56,32},{64,40},{72,48},{80,56},{88,... | collective-permute-start | bytes 393224 | tf_op jit(solution)/shard_map/ppermute | solution.py:15
  1263.8 12.4 collective-permute-start.13
  (94 other events, 1288.2 us)
where the time goes:
time: 1290 us; the launch traced here: 1280 us
  waiting for transfers between devices  349 us (27%)
  starting transfers between devices  304 us (24%)
  other arithmetic  272 us (21%)
  matrix products  187 us (14%)
  blocking collectives  94.4 us (7%)
  local copies, waits for them, and re-layouts  67.5 us (5%)
    ppermute x78, waiting for transfers between devices, shifted_2(): return lax.ppermute(block, axis, route)  349 us
    ppermute x78, starting transfers between devices, shifted_2(): return lax.ppermute(block, axis, route)  304 us
    another operation x72, other arithmetic, delta_block(): jax.scipy.linalg.solve_triangular(system, target, lower=True, unit_diagon...  217 us
    psum x1, blocking collectives, body(): gain_grad = lax.psum(gain_part, 'seq')  67.6 us
    dot_general x62, matrix products, apply_map(): jnp.einsum('hij,hjv->hiv', matrix, operand, precision=MATMUL_ACCURACY)  37 us
  transfers between devices with their start and end apart: 78, of which 66 were waited for; matrix products, arithmetic and copies ran while one was open for 2% of the time, Pallas kernels for 0%

commit v1 on v0

--- a/solution.py
+++ b/solution.py
@@ -7,6 +7,14 @@
 CH = 64
 MATMUL_ACCURACY = lax.Precision.HIGHEST
 EPSILON = 1e-06
+
+
+def doubling_sum(x, axis):
+    size, acc = (lax.axis_size(axis), x)
+    for far in [1 << k for k in range(size.bit_length() - 1)]:
+        swap = [(i, i ^ far) for i in range(size)]
+        acc = acc + lax.ppermute(acc, axis, swap)
+    return acc
 
 
 def shifted_2(block, axis, distance):
@@ -191,7 +199,7 @@
     dot_part = jnp.sum(weighted * attended, axis=(1, 2))
     gain_part = jnp.sum(value_grad * scaled, axis=0)
     dot_all = lax.psum(dot_part, "head")
-    gain_grad = lax.psum(gain_part, "seq")
+    gain_grad = doubling_sum(gain_part, "seq")
     attended_grad = (
         inverse[:, None, None] * weighted
         - attended * (inverse * inverse * inverse * dot_all / features)[:, None, None]

time: 1290 us -> 1240 us (0.961)
  blocking collectives: 94.4 us -> 26.8 us
  waiting for transfers between devices: 349 us -> 365 us
    psum x1 -> x0, blocking collectives: 67.6 us -> none  [body(): gain_grad = lax.psum(gain_part, 'seq')]
  transfers between devices with their start and end apart: 78 -> 83, of which waited for: 66 -> 71; matrix products, arithmetic and copies ran while one was open for 2% -> 2% of each run, Pallas kernels for 0% -> 0%
where the time goes in v1:
time: 1240 us; the launch traced here: 1230 us
  waiting for transfers between devices  365 us (29%)
  starting transfers between devices  307 us (25%)
  other arithmetic  273 us (22%)
  matrix products  187 us (15%)
  local copies, waits for them, and re-layouts  67.7 us (5%)
  blocking collectives  26.8 us (2%)
    ppermute x78, waiting for transfers between devices, shifted_2(): return lax.ppermute(block, axis, route)  353 us
    ppermute x78, starting transfers between devices, shifted_2(): return lax.ppermute(block, axis, route)  298 us
    another operation x72, other arithmetic, delta_block(): jax.scipy.linalg.solve_triangular(system, target, lower=True, unit_diagon...  217 us
    dot_general x62, matrix products, apply_map(): jnp.einsum('hij,hjv->hiv', matrix, operand, precision=MATMUL_ACCURACY)  37 us
  transfers between devices with their start and end apart: 83, of which 71 were waited for; matrix products, arithmetic and copies ran while one was open for 2% of the time, Pallas kernels for 0%

profile of v1, /device:TPU:162, one launch (start us, length us, event | category | flops | bytes accessed | tf_op | source)
XLA Modules:
  0.0 1230.4 jit_solution(16741582018237884326)
XLA Ops:
  59.0 14.4 %psum.14 = f32[256]{0:T(256)S(1)} all-reduce(f32[256]{0:T(256)S(1)} %get-tuple-element.2481), channel_id=1, replica_groups=mesh['seq'=32,'head'=8] {'head'}, use_global_device_ids=true, to_apply=%region_4.5 | all-reduce | flops 256 | bytes 2048 | tf_op jit(solution)/shard_map/psum | solution.py:138
  78.8 69.7 %while.136 = (s32[]{:T(128)}, f32[2,128,256]{2,1,0:T(8,128)S(1)}, f32[4,2,64]{2,1,0:T(2,128)}, f32[4,2,64,128]{3,2,1,0:T(8,128)S(1)}, f32[4,2,64]{2,1,0:T(2,128)...) while((s32[]{:T(128)}, f32[2,128,256]{2,1,0:T(8,128)S(1)}, f32[4,2,64]{2,1,0:T(2,128)}, ...), condition=%wide.region_7.8_spmd, body=%wide.region_5.0_spmd.sunk | while | flops 138780736 | bytes 1925833 | solution.py:73
  82.6 11.2 custom-call.55
  100.0 11.2 custom-call.55
  117.5 11.2 custom-call.55
  134.9 11.2 custom-call.55
  152.3 311.7 %while.137 = (s32[]{:T(128)}, f32[2,128,128]{2,1,0:T(8,128)S(1)}, f32[2,128,128]{2,1,0:T(8,128)S(1)}, f32[2,128,128]{2,1,0:T(8,128)S(1)}, s32[]{:T(128)}) while((s32[]{:T(128)}, f32[2,128,128]{2,1,0:T(8,128)S(1)}, f32[2,128,128]{2,1,0:T(8,128)S(1)}, f32[2,128,128]{2,1,0:T(8,128)S(1)}, s32[]{:T(128)}) %tuple.298), condition=%wide.region_9.10_spmd, body=%wide.region_8.9_spmd.sunk | while | flops 50364416 | bytes 1048677 | solution.py:172
  467.6 105.9 %while.139 = (s32[]{:T(128)}, f32[2,128,128]{2,1,0:T(8,128)S(1)}, bf16[4,2,64,128]{3,2,1,0:T(8,128)(2,1)}, f32[4,2,64,64]{3,2,1,0:T(8,128)}, f32[4,2,64]{2,1,0:T...) while((s32[]{:T(128)}, f32[2,128,128]{2,1,0:T(8,128)S(1)}, ...), condition=%wide.region_13.14_spmd.clone.clone, body=%wide.region_11.13_spmd.clone.clone.sunk | while | flops 126304576 | bytes 3452789 | solution.py:73
  472.0 10.6 custom-call.56
  498.5 10.6 custom-call.56
  525.0 10.6 custom-call.56
  551.4 10.6 custom-call.56
  574.1 65.0 %while.141 = (s32[]{:T(128)}, f32[2,128,128]{2,1,0:T(8,128)S(1)}, f32[4,2,1,1]{1,3,2,0:T(1,128)}, f32[4,2,64,128]{3,2,1,0:T(8,128)}, f32[4,2,64,1]{2,1,3,0:T(2,1...) while((s32[]{:T(128)}, f32[2,128,128]{2,1,0:T(8,128)S(1)}, ...), condition=%wide.region_15.17_spmd.clone, body=%wide.region_14.16_spmd.clone.sunk | while | flops 100937792 | bytes 1587911 | solution.py:73
  577.9 9.8 custom-call.59
  594.1 9.8 custom-call.59
  610.4 9.8 custom-call.59
  626.6 9.8 custom-call.59
  639.1 292.9 %while.138 = (s32[]{:T(128)}, f32[2,128,128]{2,1,0:T(8,128)S(1)}, f32[2,128,128]{2,1,0:T(8,128)S(1)}, f32[2,128,128]{2,1,0:T(8,128)S(1)}, s32[]{:T(128)}) while((s32[]{:T(128)}, f32[2,128,128]{2,1,0:T(8,128)S(1)}, f32[2,128,128]{2,1,0:T(8,128)S(1)}, f32[2,128,128]{2,1,0:T(8,128)S(1)}, s32[]{:T(128)}) %tuple.319), condition=%wide.region_17.19_spmd, body=%wide.region_16.18_spmd.sunk | while | flops 50364416 | bytes 1048677 | solution.py:195
  670.2 8.6 collective-permute-done.1
  812.5 8.7 collective-permute-done.1
  935.3 192.8 %while.140 = (s32[]{:T(128)}, f32[2,128,128]{2,1,0:T(8,128)S(1)}, f32[4,2,64,128]{3,2,1,0:T(8,128)}, f32[4,2,64,128]{3,2,1,0:T(8,128)}, bf16[4,2,64,128]{3,2,0,1...) while((s32[]{:T(128)}, f32[2,128,128]{2,1,0:T(8,128)S(1)}, ...), condition=%wide.region_29.31_spmd.clone.clone, body=%wide.region_18.30_spmd.clone.clone.sunk | while | flops 258761408 | bytes 5408265 | solution.py:73
  939.5 9.8 custom-call.58
  953.8 9.8 custom-call.57
  987.6 9.8 custom-call.58
  1001.9 9.8 custom-call.57
  1035.8 9.8 custom-call.58
  1050.1 9.8 custom-call.57
  1083.9 9.8 custom-call.58
  1098.2 9.8 custom-call.57
  1131.0 12.4 %psum.15 = f32[256]{0:T(256)S(1)} all-reduce(f32[256]{0:T(256)S(1)} %get-tuple-element.2245), channel_id=1, replica_groups=mesh['seq'=32,'head'=8] {'head'}, use_global_device_ids=true, to_apply=%region_31.33 | all-reduce | flops 256 | bytes 2048 | tf_op jit(solution)/shard_map/psum | solution.py:201
  1182.9 9.1 collective-permute-start.16
  1216.2 12.4 %collective-permute-done.12 = bf16[256,2,128]{2,0,1:T(8,128)(2,1)S(1)} collective-permute-done((bf16[256,2,128]{2,0,1:T(8,128)(2,1)S(1)}, bf16[256,2,128]{2,0,1:T(8,128)(2,1)S(1)}, u32[]{:S(2)}, u32[]{:S(2)}) %collective-permute-start.12) | collective-permute-done | bytes 131104 | tf_op jit(solution)/shard_map/ppermute | solution.py:23
  (783 shorter events, 955.6 us)
Async XLA Ops:
  1.7 32.5 %collective-permute-start.6 = (bf16[256,2,128]{2,0,1:T(8,128)(2,1)S(1)}, bf16[256,2,128]{2,0,1:T(8,128)(2,1)S(1)}, u32[]{:S(2)}, u32[]{:S(2)}) collective-permute-start(bf16[256,2,128]{2,0,1:T(8,128)(2,1)S(1)} %copy.247), channel_id=1, source_target_pairs={{0,32},{8,40},{16,48},{24,56},{32,64},{40,72},{48,80},{56,88},{64,... | collective-permute-start | bytes 393224 | tf_op jit(solution)/shard_map/ppermute | solution.py:23
  4.2 36.0 %collective-permute-start.7 = (bf16[256,2,128]{2,0,1:T(8,128)(2,1)S(1)}, bf16[256,2,128]{2,0,1:T(8,128)(2,1)S(1)}, u32[]{:S(2)}, u32[]{:S(2)}) collective-permute-start(bf16[256,2,128]{2,0,1:T(8,128)(2,1)S(1)} %copy.247), channel_id=1, source_target_pairs={{0,24},{8,32},{16,40},{24,48},{32,56},{40,64},{48,72},{56,80},{64,... | collective-permute-start | bytes 393224 | tf_op jit(solution)/shard_map/ppermute | solution.py:23
  11.9 30.7 %collective-permute-start.8 = (bf16[256,2,128]{2,0,1:T(8,128)(2,1)S(1)}, bf16[256,2,128]{2,0,1:T(8,128)(2,1)S(1)}, u32[]{:S(2)}, u32[]{:S(2)}) collective-permute-start(bf16[256,2,128]{2,0,1:T(8,128)(2,1)S(1)} %copy.247), channel_id=1, source_target_pairs={{0,16},{8,24},{16,32},{24,40},{32,48},{40,56},{48,64},{56,72},{64,... | collective-permute-start | bytes 393224 | tf_op jit(solution)/shard_map/ppermute | solution.py:23
  15.3 29.8 %collective-permute-start.9 = (bf16[256,2,128]{2,0,1:T(8,128)(2,1)S(1)}, bf16[256,2,128]{2,0,1:T(8,128)(2,1)S(1)}, u32[]{:S(2)}, u32[]{:S(2)}) collective-permute-start(bf16[256,2,128]{2,0,1:T(8,128)(2,1)S(1)} %copy.247), channel_id=1, source_target_pairs={{0,8},{8,16},{16,24},{24,32},{32,40},{40,48},{48,56},{56,64},{64,7... | collective-permute-start | bytes 393224 | tf_op jit(solution)/shard_map/ppermute | solution.py:23
  30.2 17.6 %collective-permute-start.2 = (bf16[256,2,128]{0,2,1:T(8,128)(2,1)S(1)}, bf16[256,2,128]{0,2,1:T(8,128)(2,1)S(1)}, u32[]{:S(2)}, u32[]{:S(2)}) collective-permute-start(bf16[256,2,128]{0,2,1:T(8,128)(2,1)S(1)} %copy.242), channel_id=1, source_target_pairs={{0,32},{8,40},{16,48},{24,56},{32,64},{40,72},{48,80},{56,88},{64,... | collective-permute-start | bytes 393224 | tf_op jit(solution)/shard_map/ppermute | solution.py:23
  34.2 15.9 %collective-permute-start.3 = (bf16[256,2,128]{0,2,1:T(8,128)(2,1)S(1)}, bf16[256,2,128]{0,2,1:T(8,128)(2,1)S(1)}, u32[]{:S(2)}, u32[]{:S(2)}) collective-permute-start(bf16[256,2,128]{0,2,1:T(8,128)(2,1)S(1)} %copy.242), channel_id=1, source_target_pairs={{0,24},{8,32},{16,40},{24,48},{32,56},{40,64},{48,72},{56,80},{64,... | collective-permute-start | bytes 393224 | tf_op jit(solution)/shard_map/ppermute | solution.py:23
  40.2 16.7 %collective-permute-start.4 = (bf16[256,2,128]{0,2,1:T(8,128)(2,1)S(1)}, bf16[256,2,128]{0,2,1:T(8,128)(2,1)S(1)}, u32[]{:S(2)}, u32[]{:S(2)}) collective-permute-start(bf16[256,2,128]{0,2,1:T(8,128)(2,1)S(1)} %copy.242), channel_id=1, source_target_pairs={{0,16},{8,24},{16,32},{24,40},{32,48},{40,56},{48,64},{56,72},{64,... | collective-permute-start | bytes 393224 | tf_op jit(solution)/shard_map/ppermute | solution.py:23
  42.6 15.2 %collective-permute-start.5 = (bf16[256,2,128]{0,2,1:T(8,128)(2,1)S(1)}, bf16[256,2,128]{0,2,1:T(8,128)(2,1)S(1)}, u32[]{:S(2)}, u32[]{:S(2)}) collective-permute-start(bf16[256,2,128]{0,2,1:T(8,128)(2,1)S(1)} %copy.242), channel_id=1, source_target_pairs={{0,8},{8,16},{16,24},{24,32},{32,40},{40,48},{48,56},{56,64},{64,7... | collective-permute-start | bytes 393224 | tf_op jit(solution)/shard_map/ppermute | solution.py:23
  199.0 9.4 collective-permute-start
  279.3 10.0 collective-permute-start
  290.2 10.5 collective-permute-start
  362.3 9.6 collective-permute-start
  372.8 10.6 collective-permute-start
  639.4 9.3 collective-permute-start.1
  649.0 9.3 collective-permute-start.1
  658.6 9.4 collective-permute-start.1
  668.2 10.5 collective-permute-start.1
  679.0 10.0 collective-permute-start.1
  734.6 9.6 collective-permute-start.1
  744.5 10.3 collective-permute-start.1
  755.1 9.3 collective-permute-start.1
  810.6 10.6 collective-permute-start.1
  821.4 9.7 collective-permute-start.1
  1177.7 16.2 %collective-permute-start.21 = (f32[2,128]{1,0:T(2,128)S(1)}, f32[2,128]{1,0:T(2,128)S(1)}, u32[]{:S(2)}, u32[]{:S(2)}) collective-permute-start(f32[2,128]{1,0:T(2,128)S(1)} %add.282), channel_id=1, source_target_pairs={{0,64},{8,72},{16,80},{24,88},{32,96},{40,104},{48,112},{56,120},{... | collective-permute-start | bytes 3080 | tf_op jit(solution)/shard_map/ppermute | solution.py:16
  1178.5 23.2 %collective-permute-start.14 = (bf16[256,2,128]{0,2,1:T(8,128)(2,1)S(1)}, bf16[256,2,128]{0,2,1:T(8,128)(2,1)S(1)}, u32[]{:S(2)}, u32[]{:S(2)}) collective-permute-start(bf16[256,2,128]{0,2,1:T(8,128)(2,1)S(1)} %get-tuple-element.2469), channel_id=1, source_target_pairs={{8,0},{16,8},{24,16},{32,24},{40,32},{48,40},{56,48},{64,56},{72,6... | collective-permute-start | bytes 393224 | tf_op jit(solution)/shard_map/ppermute | solution.py:23
  1180.4 25.8 %collective-permute-start.15 = (bf16[256,2,128]{0,2,1:T(8,128)(2,1)S(1)}, bf16[256,2,128]{0,2,1:T(8,128)(2,1)S(1)}, u32[]{:S(2)}, u32[]{:S(2)}) collective-permute-start(bf16[256,2,128]{0,2,1:T(8,128)(2,1)S(1)} %get-tuple-element.2472), channel_id=1, source_target_pairs={{16,0},{24,8},{32,16},{40,24},{48,32},{56,40},{64,48},{72,56},{80,... | collective-permute-start | bytes 393224 | tf_op jit(solution)/shard_map/ppermute | solution.py:23
  1182.9 29.2 %collective-permute-start.16 = (bf16[256,2,128]{0,2,1:T(8,128)(2,1)S(1)}, bf16[256,2,128]{0,2,1:T(8,128)(2,1)S(1)}, u32[]{:S(2)}, u32[]{:S(2)}) collective-permute-start(bf16[256,2,128]{0,2,1:T(8,128)(2,1)S(1)} %get-tuple-element.2471), channel_id=1, source_target_pairs={{24,0},{32,8},{40,16},{48,24},{56,32},{64,40},{72,48},{80,56},{88,... | collective-permute-start | bytes 393224 | tf_op jit(solution)/shard_map/ppermute | solution.py:23
  1192.0 22.0 %collective-permute-start.17 = (bf16[256,2,128]{0,2,1:T(8,128)(2,1)S(1)}, bf16[256,2,128]{0,2,1:T(8,128)(2,1)S(1)}, u32[]{:S(2)}, u32[]{:S(2)}) collective-permute-start(bf16[256,2,128]{0,2,1:T(8,128)(2,1)S(1)} %get-tuple-element.2470), channel_id=1, source_target_pairs={{32,0},{40,8},{48,16},{56,24},{64,32},{72,40},{80,48},{88,56},{96,... | collective-permute-start | bytes 393224 | tf_op jit(solution)/shard_map/ppermute | solution.py:23
  1199.1 16.7 %collective-permute-start.10 = (bf16[256,2,128]{2,0,1:T(8,128)(2,1)S(1)}, bf16[256,2,128]{2,0,1:T(8,128)(2,1)S(1)}, u32[]{:S(2)}, u32[]{:S(2)}) collective-permute-start(bf16[256,2,128]{2,0,1:T(8,128)(2,1)S(1)} %get-tuple-element.2473), channel_id=1, source_target_pairs={{8,0},{16,8},{24,16},{32,24},{40,32},{48,40},{56,48},{64,56},{72,6... | collective-permute-start | bytes 393224 | tf_op jit(solution)/shard_map/ppermute | solution.py:23
  1201.7 14.5 %collective-permute-start.11 = (bf16[256,2,128]{2,0,1:T(8,128)(2,1)S(1)}, bf16[256,2,128]{2,0,1:T(8,128)(2,1)S(1)}, u32[]{:S(2)}, u32[]{:S(2)}) collective-permute-start(bf16[256,2,128]{2,0,1:T(8,128)(2,1)S(1)} %get-tuple-element.2476), channel_id=1, source_target_pairs={{16,0},{24,8},{32,16},{40,24},{48,32},{56,40},{64,48},{72,56},{80,... | collective-permute-start | bytes 393224 | tf_op jit(solution)/shard_map/ppermute | solution.py:23
  1206.2 22.4 %collective-permute-start.12 = (bf16[256,2,128]{2,0,1:T(8,128)(2,1)S(1)}, bf16[256,2,128]{2,0,1:T(8,128)(2,1)S(1)}, u32[]{:S(2)}, u32[]{:S(2)}) collective-permute-start(bf16[256,2,128]{2,0,1:T(8,128)(2,1)S(1)} %get-tuple-element.2475), channel_id=1, source_target_pairs={{24,0},{32,8},{40,16},{48,24},{56,32},{64,40},{72,48},{80,56},{88,... | collective-permute-start | bytes 393224 | tf_op jit(solution)/shard_map/ppermute | solution.py:23
  1212.1 16.5 %collective-permute-start.13 = (bf16[256,2,128]{2,0,1:T(8,128)(2,1)S(1)}, bf16[256,2,128]{2,0,1:T(8,128)(2,1)S(1)}, u32[]{:S(2)}, u32[]{:S(2)}) collective-permute-start(bf16[256,2,128]{2,0,1:T(8,128)(2,1)S(1)} %get-tuple-element.2474), channel_id=1, source_target_pairs={{32,0},{40,8},{48,16},{56,24},{64,32},{72,40},{80,48},{88,56},{96,... | collective-permute-start | bytes 393224 | tf_op jit(solution)/shard_map/ppermute | solution.py:23
  (99 other events, 1122.1 us)
